TPU v7x, 256 devices: a whole 4x4x8 slice. The times are simulated.
256 devices in a mesh: req: 64 (over y, z_lo, x, core), tp: 4 (over z_hi).
Axes of the slice: x: 4, y: 4, z: 8 (z_hi: 4, z_lo: 2; z = z_hi * 2 + z_lo), core: 2. Of those that a mesh axis runs over, the one named last changes fastest.
Arguments:
- tokens: bfloat16 [16384, 2048], P('req'), may hold values from -6 to 6
- norm_gain: float32 [2048], replicated, may hold values from 0.25 to 1.75
- w_query: bfloat16 [2048, 2048], P(None, 'tp'), may hold values from -1 to 1
- w_key: bfloat16 [2048, 2048], P(None, 'tp'), may hold values from -1 to 1
- w_value: bfloat16 [2048, 2048], P(None, 'tp'), may hold values from -0.125 to 0.125
- w_out: bfloat16 [2048, 2048], P('tp'), may hold values from -0.125 to 0.125
- lambdas: float32 [4, 8, 128], P(None, 'tp'), may hold values from -1 to 1
- sub_gain: float32 [8, 256], P('tp'), may hold values from 0.5 to 2
- lengths: int32 [4], replicated, may hold values from 1 to 8192, 16384 in all
Outputs:
- hidden: bfloat16 [16384, 2048], P('req')
- key_cache: bfloat16 [16384, 2048], P('req', 'tp')
- value_cache: bfloat16 [16384, 2048], P('req', 'tp')
Inputs may be any that keep to these rules, and one draw needn't show every extreme that they name: The lengths sum to 16384; the longest is exactly 8192.
All inputs are finite; a program needn't handle non-finite values.
Results may differ from a plain program's by a relative error of at most 0.007.
Values may be sent and summed in bfloat16 or wider, within the bound.
No kernel may reach another device: no remote copies, remote signals or barrier semaphores. Data moves between devices by JAX's collectives and lax.ppermute only.
A program may use at most 128 MiB of HBM per device.

v0:
```python
import math
import jax
import jax.numpy as jnp
from jax import lax
from jax.sharding import PartitionSpec as P

QK = 128
VD = 256
lambda_start = 0.8 - 0.6 * math.exp(-3.3)
masked_score = -1e30


def shifted(value, axis, steps):
    count = lax.axis_size(axis)
    first, last = (max(0, -steps), min(count, count - steps))
    return lax.ppermute(value, axis, [(source, source + steps) for source in range(first, last)])


def locate(index, lengths):
    ends = jnp.cumsum(lengths)
    starts = ends - lengths
    segment = jnp.sum((ends[None, :] <= index[:, None]).astype(jnp.int32), axis=1)
    hit = jnp.arange(lengths.shape[0], dtype=jnp.int32)[None, :] == segment[:, None]
    begin = jnp.sum(jnp.where(hit, starts[None, :], 0), axis=1)
    return (segment, index - begin)


def rotate(proj, position):
    half = proj.shape[-1] // 2
    freq = 10000.0 ** (-jnp.arange(half, dtype=jnp.float32) / half)
    angle = position.astype(jnp.float32)[:, None] * freq[None, :]
    cosine = jnp.cos(angle)[:, None, None, :]
    sine = jnp.sin(angle)[:, None, None, :]
    front = proj[..., :half]
    back = proj[..., half:]
    return jnp.concatenate([front * cosine - back * sine, back * cosine + front * sine], axis=-1)


def on_device(tokens, norm_gain, w_query, w_key, w_value, w_out, lambdas, sub_gain, lengths):
    rows = tokens.shape[0]
    heads = w_query.shape[1] // (2 * QK)
    key_cols = heads * 2 * QK
    total = rows * lax.axis_size("req")
    longest = min(8192, total // 2)
    reach = longest // rows
    first = lax.axis_index("req") * rows
    local_index = first + jnp.arange(rows, dtype=jnp.int32)
    seg_query, pos_query = locate(local_index, lengths)
    xf = tokens.astype(jnp.float32)
    normed = (xf * lax.rsqrt(jnp.mean(xf * xf, axis=-1, keepdims=True) + 1e-06) * norm_gain).astype(
        jnp.bfloat16
    )
    query = rotate(
        jnp.dot(normed, w_query, preferred_element_type=jnp.float32).reshape(rows, heads, 2, QK),
        pos_query,
    ).astype(jnp.bfloat16)
    keys = rotate(
        jnp.dot(normed, w_key, preferred_element_type=jnp.float32).reshape(rows, heads, 2, QK),
        pos_query,
    ).astype(jnp.bfloat16)
    values = jnp.dot(normed, w_value, preferred_element_type=jnp.float32).astype(jnp.bfloat16)
    key_flat = keys.reshape(rows, key_cols)
    own = jnp.concatenate([key_flat, values], axis=1)
    lam = (
        jnp.exp(jnp.sum(lambdas[0] * lambdas[1], axis=-1))
        - jnp.exp(jnp.sum(lambdas[2] * lambdas[3], axis=-1))
        + lambda_start
    )
    scale = QK ** (-0.5)

    def absorb(state, shard, anchor):
        key_index = anchor + jnp.arange(rows, dtype=jnp.int32)
        key_seg, unused = locate(key_index, lengths)
        allowed = (
            (key_index >= 0)[None, :]
            & (key_index[None, :] <= local_index[:, None])
            & (key_seg[None, :] == seg_query[:, None])
        )

        def compute(carry):
            top, mass, acc = carry
            shard_keys = shard[:, :key_cols].reshape(rows, heads, 2, QK)
            shard_values = shard[:, key_cols:].reshape(rows, heads, VD)
            scores = (
                jnp.einsum("qhmd,khmd->mhqk", query, shard_keys, preferred_element_type=jnp.float32)
                * scale
            )
            scores = jnp.where(allowed, scores, masked_score)
            new_top = jnp.maximum(top, jnp.max(scores, axis=-1))
            weights = jnp.where(allowed, jnp.exp(scores - new_top[..., None]), 0.0)
            fade = jnp.exp(top - new_top)
            mass = mass * fade + jnp.sum(weights, axis=-1)
            acc = acc * fade[..., None] + jnp.einsum(
                "mhqk,khv->mhqv",
                weights.astype(jnp.bfloat16),
                shard_values,
                preferred_element_type=jnp.float32,
            )
            return (new_top, mass, acc)

        def keep(carry):
            return carry

        return lax.cond(jnp.any(allowed), compute, keep, state)

    start = (
        jnp.full((2, heads, rows), masked_score, jnp.float32),
        jnp.zeros((2, heads, rows), jnp.float32),
        jnp.zeros((2, heads, rows, VD), jnp.float32),
    )
    arriving = shifted(own, "req", 1)
    state = absorb(start, own, first)

    def turn(step, carry):
        current, moving = carry
        following = shifted(moving, "req", 1)
        return (absorb(current, moving, first - (step + 1) * rows), following)

    state, moving = lax.fori_loop(0, reach - 1, turn, (state, arriving))
    state = absorb(state, moving, first - reach * rows)
    top, mass, acc = state
    attended = acc / mass[..., None]
    diff = attended[0] - lam[:, None, None] * attended[1]
    normed_heads = (
        diff
        * lax.rsqrt(jnp.mean(diff * diff, axis=-1, keepdims=True) + 1e-05)
        * sub_gain[:, None, :]
        * (1.0 - lambda_start)
    )
    merged = jnp.transpose(normed_heads, (1, 0, 2)).reshape(rows, heads * VD).astype(jnp.bfloat16)
    summed = lax.psum(
        jnp.dot(merged, w_out, preferred_element_type=jnp.float32).astype(jnp.bfloat16), "tp"
    ).astype(jnp.float32)
    hidden = (xf + summed).astype(jnp.bfloat16)
    return (hidden, key_flat, values)


def solution(mesh):
    in_specs = (
        P("req", None),
        P(),
        P(None, "tp"),
        P(None, "tp"),
        P(None, "tp"),
        P("tp", None),
        P(None, "tp", None),
        P("tp", None),
        P(),
    )
    out_specs = (P("req", None), P("req", "tp"), P("req", "tp"))
    return jax.shard_map(
        on_device, mesh=mesh, in_specs=in_specs, out_specs=out_specs, check_vma=False
    )
```

profile of v0, /device:TPU:1, one launch (start us, length us, event | category | flops | bytes accessed | tf_op | source)
XLA Modules:
  0.0 609.4 jit_solution(146816331163059637)
XLA Ops:
  32.9 7.5 %conditional.3 = (f32[2,2,256]{2,1,0:T(2,128)}, f32[2,2,256]{2,1,0:T(2,128)S(1)}, f32[2,2,256,256]{3,2,0,1:T(8,128)S(1)}) conditional(s32[]{:T(128)} %convert_element_type.87, () %tuple.51, (pred[256,256]{0,1:T(8,128)(4,1)S(1)}, bf16[256,2,2,128]{3,0,1,2:T(8,128)(2,1)S(1)}, bf16[256,2,2,128]{3,0,1,2:T(8,128)(2,1)}, bf16[256,512]{1,0:T(8,128)(2,1)}) %tuple.125), branch_computations={%region_7.8_spmd, %region_8.11_spmd} | conditional | flops 203427840 | bytes 5685272 | solution.py:104
  42.7 417.4 %while.23 = (s32[]{:T(128)}, f32[2,2,256]{2,1,0:T(2,128)}, f32[2,2,256]{2,1,0:T(2,128)S(1)}, f32[2,2,256,256]{3,2,0,1:T(8,128)S(1)}, bf16[256,1024]{0,1:T(8,128)...) while((s32[]{:T(128)}, f32[2,2,256]{2,1,0:T(2,128)}, ...), condition=%wide.region_19.20_spmd.clone.clone, body=%wide.region_12.19_spmd.clone.clone.sunk | while | flops 204019456 | bytes 10498871 | solution.py:119
  73.3 4.9 collective-permute-done
  98.7 4.9 collective-permute-done
  124.0 4.9 collective-permute-done
  149.4 4.9 collective-permute-done
  162.1 4.9 collective-permute-done
  174.7 4.9 collective-permute-done
  187.4 4.9 collective-permute-done
  200.1 4.9 collective-permute-done
  270.2 6.0 collective-permute-start
  284.5 6.5 %collective-permute-start = (bf16[256,1024]{0,1:T(8,128)(2,1)}, bf16[256,1024]{0,1:T(8,128)(2,1)}, u32[]{:S(2)}, u32[]{:S(2)}) collective-permute-start(bf16[256,1024]{0,1:T(8,128)(2,1)} %copy.132), channel_id=1, source_target_pairs={{0,4},{4,8},{8,12},{12,16},{16,20},{20,24},{24,28},{28,32},{32,36}... | collective-permute-start | bytes 1572872 | tf_op jit(solution)/shard_map/while/body/eval_jaxpr/ppermute | solution.py:16
  299.3 6.5 %collective-permute-start = (bf16[256,1024]{0,1:T(8,128)(2,1)}, bf16[256,1024]{0,1:T(8,128)(2,1)}, u32[]{:S(2)}, u32[]{:S(2)}) collective-permute-start(bf16[256,1024]{0,1:T(8,128)(2,1)} %copy.132), channel_id=1, source_target_pairs={{0,4},{4,8},{8,12},{12,16},{16,20},{20,24},{24,28},{28,32},{32,36}... | collective-permute-start | bytes 1572872 | tf_op jit(solution)/shard_map/while/body/eval_jaxpr/ppermute | solution.py:16
  314.1 6.5 %collective-permute-start = (bf16[256,1024]{0,1:T(8,128)(2,1)}, bf16[256,1024]{0,1:T(8,128)(2,1)}, u32[]{:S(2)}, u32[]{:S(2)}) collective-permute-start(bf16[256,1024]{0,1:T(8,128)(2,1)} %copy.132), channel_id=1, source_target_pairs={{0,4},{4,8},{8,12},{12,16},{16,20},{20,24},{24,28},{28,32},{32,36}... | collective-permute-start | bytes 1572872 | tf_op jit(solution)/shard_map/while/body/eval_jaxpr/ppermute | solution.py:16
  328.9 6.5 %collective-permute-start = (bf16[256,1024]{0,1:T(8,128)(2,1)}, bf16[256,1024]{0,1:T(8,128)(2,1)}, u32[]{:S(2)}, u32[]{:S(2)}) collective-permute-start(bf16[256,1024]{0,1:T(8,128)(2,1)} %copy.132), channel_id=1, source_target_pairs={{0,4},{4,8},{8,12},{12,16},{16,20},{20,24},{24,28},{28,32},{32,36}... | collective-permute-start | bytes 1572872 | tf_op jit(solution)/shard_map/while/body/eval_jaxpr/ppermute | solution.py:16
  343.7 6.5 %collective-permute-start = (bf16[256,1024]{0,1:T(8,128)(2,1)}, bf16[256,1024]{0,1:T(8,128)(2,1)}, u32[]{:S(2)}, u32[]{:S(2)}) collective-permute-start(bf16[256,1024]{0,1:T(8,128)(2,1)} %copy.132), channel_id=1, source_target_pairs={{0,4},{4,8},{8,12},{12,16},{16,20},{20,24},{24,28},{28,32},{32,36}... | collective-permute-start | bytes 1572872 | tf_op jit(solution)/shard_map/while/body/eval_jaxpr/ppermute | solution.py:16
  358.4 6.5 %collective-permute-start = (bf16[256,1024]{0,1:T(8,128)(2,1)}, bf16[256,1024]{0,1:T(8,128)(2,1)}, u32[]{:S(2)}, u32[]{:S(2)}) collective-permute-start(bf16[256,1024]{0,1:T(8,128)(2,1)} %copy.132), channel_id=1, source_target_pairs={{0,4},{4,8},{8,12},{12,16},{16,20},{20,24},{24,28},{28,32},{32,36}... | collective-permute-start | bytes 1572872 | tf_op jit(solution)/shard_map/while/body/eval_jaxpr/ppermute | solution.py:16
  373.2 6.5 %collective-permute-start = (bf16[256,1024]{0,1:T(8,128)(2,1)}, bf16[256,1024]{0,1:T(8,128)(2,1)}, u32[]{:S(2)}, u32[]{:S(2)}) collective-permute-start(bf16[256,1024]{0,1:T(8,128)(2,1)} %copy.132), channel_id=1, source_target_pairs={{0,4},{4,8},{8,12},{12,16},{16,20},{20,24},{24,28},{28,32},{32,36}... | collective-permute-start | bytes 1572872 | tf_op jit(solution)/shard_map/while/body/eval_jaxpr/ppermute | solution.py:16
  388.0 6.5 %collective-permute-start = (bf16[256,1024]{0,1:T(8,128)(2,1)}, bf16[256,1024]{0,1:T(8,128)(2,1)}, u32[]{:S(2)}, u32[]{:S(2)}) collective-permute-start(bf16[256,1024]{0,1:T(8,128)(2,1)} %copy.132), channel_id=1, source_target_pairs={{0,4},{4,8},{8,12},{12,16},{16,20},{20,24},{24,28},{28,32},{32,36}... | collective-permute-start | bytes 1572872 | tf_op jit(solution)/shard_map/while/body/eval_jaxpr/ppermute | solution.py:16
  402.8 6.5 %collective-permute-start = (bf16[256,1024]{0,1:T(8,128)(2,1)}, bf16[256,1024]{0,1:T(8,128)(2,1)}, u32[]{:S(2)}, u32[]{:S(2)}) collective-permute-start(bf16[256,1024]{0,1:T(8,128)(2,1)} %copy.132), channel_id=1, source_target_pairs={{0,4},{4,8},{8,12},{12,16},{16,20},{20,24},{24,28},{28,32},{32,36}... | collective-permute-start | bytes 1572872 | tf_op jit(solution)/shard_map/while/body/eval_jaxpr/ppermute | solution.py:16
  417.6 6.5 %collective-permute-start = (bf16[256,1024]{0,1:T(8,128)(2,1)}, bf16[256,1024]{0,1:T(8,128)(2,1)}, u32[]{:S(2)}, u32[]{:S(2)}) collective-permute-start(bf16[256,1024]{0,1:T(8,128)(2,1)} %copy.132), channel_id=1, source_target_pairs={{0,4},{4,8},{8,12},{12,16},{16,20},{20,24},{24,28},{28,32},{32,36}... | collective-permute-start | bytes 1572872 | tf_op jit(solution)/shard_map/while/body/eval_jaxpr/ppermute | solution.py:16
  432.4 6.5 %collective-permute-start = (bf16[256,1024]{0,1:T(8,128)(2,1)}, bf16[256,1024]{0,1:T(8,128)(2,1)}, u32[]{:S(2)}, u32[]{:S(2)}) collective-permute-start(bf16[256,1024]{0,1:T(8,128)(2,1)} %copy.132), channel_id=1, source_target_pairs={{0,4},{4,8},{8,12},{12,16},{16,20},{20,24},{24,28},{28,32},{32,36}... | collective-permute-start | bytes 1572872 | tf_op jit(solution)/shard_map/while/body/eval_jaxpr/ppermute | solution.py:16
  447.1 6.5 %collective-permute-start = (bf16[256,1024]{0,1:T(8,128)(2,1)}, bf16[256,1024]{0,1:T(8,128)(2,1)}, u32[]{:S(2)}, u32[]{:S(2)}) collective-permute-start(bf16[256,1024]{0,1:T(8,128)(2,1)} %copy.132), channel_id=1, source_target_pairs={{0,4},{4,8},{8,12},{12,16},{16,20},{20,24},{24,28},{28,32},{32,36}... | collective-permute-start | bytes 1572872 | tf_op jit(solution)/shard_map/while/body/eval_jaxpr/ppermute | solution.py:16
  464.8 135.1 %all-reduce.2.cloned.1.call-done = bf16[256,2048]{1,0:T(8,128)(2,1)} async-done(((bf16[256,2048]{1,0:T(8,128)(2,1)}), bf16[256,2048]{1,0:T(8,128)(2,1)}) %all-reduce.2.cloned.1.call-update) | async-done | bytes 1048592 | tf_op jit(solution)/shard_map/psum | solution.py:131
  (345 shorter events, 322.1 us)
Async XLA Ops:
  7.2 592.7 %all-reduce.2.cloned.1.call-start = ((), (), s32[]{:S(2)}) async-start(), calls=%async_computation | async-start | bytes 2097152 | tf_op jit(solution)/shard_map/psum | solution.py:131
  21.9 18.7 %collective-permute-start.1 = (bf16[256,1024]{1,0:T(8,128)(2,1)}, bf16[256,1024]{1,0:T(8,128)(2,1)}, u32[]{:S(2)}, u32[]{:S(2)}) collective-permute-start(bf16[256,1024]{1,0:T(8,128)(2,1)} %pad_maximum_fusion), channel_id=1, source_target_pairs={{0,4},{4,8},{8,12},{12,16},{16,20},{20,24},{24,28},{28,32},{32,36}... | collective-permute-start | bytes 1572872 | tf_op jit(solution)/shard_map/ppermute | solution.py:16
  54.8 10.8 %collective-permute-start = (bf16[256,1024]{0,1:T(8,128)(2,1)}, bf16[256,1024]{0,1:T(8,128)(2,1)}, u32[]{:S(2)}, u32[]{:S(2)}) collective-permute-start(bf16[256,1024]{0,1:T(8,128)(2,1)} %copy.132), channel_id=1, source_target_pairs={{0,4},{4,8},{8,12},{12,16},{16,20},{20,24},{24,28},{28,32},{32,36}... | collective-permute-start | bytes 1572872 | tf_op jit(solution)/shard_map/while/body/eval_jaxpr/ppermute | solution.py:16
  67.4 10.8 %collective-permute-start = (bf16[256,1024]{0,1:T(8,128)(2,1)}, bf16[256,1024]{0,1:T(8,128)(2,1)}, u32[]{:S(2)}, u32[]{:S(2)}) collective-permute-start(bf16[256,1024]{0,1:T(8,128)(2,1)} %copy.132), channel_id=1, source_target_pairs={{0,4},{4,8},{8,12},{12,16},{16,20},{20,24},{24,28},{28,32},{32,36}... | collective-permute-start | bytes 1572872 | tf_op jit(solution)/shard_map/while/body/eval_jaxpr/ppermute | solution.py:16
  92.8 10.8 %collective-permute-start = (bf16[256,1024]{0,1:T(8,128)(2,1)}, bf16[256,1024]{0,1:T(8,128)(2,1)}, u32[]{:S(2)}, u32[]{:S(2)}) collective-permute-start(bf16[256,1024]{0,1:T(8,128)(2,1)} %copy.132), channel_id=1, source_target_pairs={{0,4},{4,8},{8,12},{12,16},{16,20},{20,24},{24,28},{28,32},{32,36}... | collective-permute-start | bytes 1572872 | tf_op jit(solution)/shard_map/while/body/eval_jaxpr/ppermute | solution.py:16
  118.1 10.8 %collective-permute-start = (bf16[256,1024]{0,1:T(8,128)(2,1)}, bf16[256,1024]{0,1:T(8,128)(2,1)}, u32[]{:S(2)}, u32[]{:S(2)}) collective-permute-start(bf16[256,1024]{0,1:T(8,128)(2,1)} %copy.132), channel_id=1, source_target_pairs={{0,4},{4,8},{8,12},{12,16},{16,20},{20,24},{24,28},{28,32},{32,36}... | collective-permute-start | bytes 1572872 | tf_op jit(solution)/shard_map/while/body/eval_jaxpr/ppermute | solution.py:16
  156.2 10.8 %collective-permute-start = (bf16[256,1024]{0,1:T(8,128)(2,1)}, bf16[256,1024]{0,1:T(8,128)(2,1)}, u32[]{:S(2)}, u32[]{:S(2)}) collective-permute-start(bf16[256,1024]{0,1:T(8,128)(2,1)} %copy.132), channel_id=1, source_target_pairs={{0,4},{4,8},{8,12},{12,16},{16,20},{20,24},{24,28},{28,32},{32,36}... | collective-permute-start | bytes 1572872 | tf_op jit(solution)/shard_map/while/body/eval_jaxpr/ppermute | solution.py:16
  181.5 10.8 %collective-permute-start = (bf16[256,1024]{0,1:T(8,128)(2,1)}, bf16[256,1024]{0,1:T(8,128)(2,1)}, u32[]{:S(2)}, u32[]{:S(2)}) collective-permute-start(bf16[256,1024]{0,1:T(8,128)(2,1)} %copy.132), channel_id=1, source_target_pairs={{0,4},{4,8},{8,12},{12,16},{16,20},{20,24},{24,28},{28,32},{32,36}... | collective-permute-start | bytes 1572872 | tf_op jit(solution)/shard_map/while/body/eval_jaxpr/ppermute | solution.py:16
  206.9 10.8 %collective-permute-start = (bf16[256,1024]{0,1:T(8,128)(2,1)}, bf16[256,1024]{0,1:T(8,128)(2,1)}, u32[]{:S(2)}, u32[]{:S(2)}) collective-permute-start(bf16[256,1024]{0,1:T(8,128)(2,1)} %copy.132), channel_id=1, source_target_pairs={{0,4},{4,8},{8,12},{12,16},{16,20},{20,24},{24,28},{28,32},{32,36}... | collective-permute-start | bytes 1572872 | tf_op jit(solution)/shard_map/while/body/eval_jaxpr/ppermute | solution.py:16
  232.2 10.8 %collective-permute-start = (bf16[256,1024]{0,1:T(8,128)(2,1)}, bf16[256,1024]{0,1:T(8,128)(2,1)}, u32[]{:S(2)}, u32[]{:S(2)}) collective-permute-start(bf16[256,1024]{0,1:T(8,128)(2,1)} %copy.132), channel_id=1, source_target_pairs={{0,4},{4,8},{8,12},{12,16},{16,20},{20,24},{24,28},{28,32},{32,36}... | collective-permute-start | bytes 1572872 | tf_op jit(solution)/shard_map/while/body/eval_jaxpr/ppermute | solution.py:16
  257.6 10.8 %collective-permute-start = (bf16[256,1024]{0,1:T(8,128)(2,1)}, bf16[256,1024]{0,1:T(8,128)(2,1)}, u32[]{:S(2)}, u32[]{:S(2)}) collective-permute-start(bf16[256,1024]{0,1:T(8,128)(2,1)} %copy.132), channel_id=1, source_target_pairs={{0,4},{4,8},{8,12},{12,16},{16,20},{20,24},{24,28},{28,32},{32,36}... | collective-permute-start | bytes 1572872 | tf_op jit(solution)/shard_map/while/body/eval_jaxpr/ppermute | solution.py:16
  270.2 12.4 %collective-permute-start = (bf16[256,1024]{0,1:T(8,128)(2,1)}, bf16[256,1024]{0,1:T(8,128)(2,1)}, u32[]{:S(2)}, u32[]{:S(2)}) collective-permute-start(bf16[256,1024]{0,1:T(8,128)(2,1)} %copy.132), channel_id=1, source_target_pairs={{0,4},{4,8},{8,12},{12,16},{16,20},{20,24},{24,28},{28,32},{32,36}... | collective-permute-start | bytes 1572872 | tf_op jit(solution)/shard_map/while/body/eval_jaxpr/ppermute | solution.py:16
  284.5 12.9 %collective-permute-start = (bf16[256,1024]{0,1:T(8,128)(2,1)}, bf16[256,1024]{0,1:T(8,128)(2,1)}, u32[]{:S(2)}, u32[]{:S(2)}) collective-permute-start(bf16[256,1024]{0,1:T(8,128)(2,1)} %copy.132), channel_id=1, source_target_pairs={{0,4},{4,8},{8,12},{12,16},{16,20},{20,24},{24,28},{28,32},{32,36}... | collective-permute-start | bytes 1572872 | tf_op jit(solution)/shard_map/while/body/eval_jaxpr/ppermute | solution.py:16
  299.3 12.9 %collective-permute-start = (bf16[256,1024]{0,1:T(8,128)(2,1)}, bf16[256,1024]{0,1:T(8,128)(2,1)}, u32[]{:S(2)}, u32[]{:S(2)}) collective-permute-start(bf16[256,1024]{0,1:T(8,128)(2,1)} %copy.132), channel_id=1, source_target_pairs={{0,4},{4,8},{8,12},{12,16},{16,20},{20,24},{24,28},{28,32},{32,36}... | collective-permute-start | bytes 1572872 | tf_op jit(solution)/shard_map/while/body/eval_jaxpr/ppermute | solution.py:16
  314.1 12.9 %collective-permute-start = (bf16[256,1024]{0,1:T(8,128)(2,1)}, bf16[256,1024]{0,1:T(8,128)(2,1)}, u32[]{:S(2)}, u32[]{:S(2)}) collective-permute-start(bf16[256,1024]{0,1:T(8,128)(2,1)} %copy.132), channel_id=1, source_target_pairs={{0,4},{4,8},{8,12},{12,16},{16,20},{20,24},{24,28},{28,32},{32,36}... | collective-permute-start | bytes 1572872 | tf_op jit(solution)/shard_map/while/body/eval_jaxpr/ppermute | solution.py:16
  328.9 12.9 %collective-permute-start = (bf16[256,1024]{0,1:T(8,128)(2,1)}, bf16[256,1024]{0,1:T(8,128)(2,1)}, u32[]{:S(2)}, u32[]{:S(2)}) collective-permute-start(bf16[256,1024]{0,1:T(8,128)(2,1)} %copy.132), channel_id=1, source_target_pairs={{0,4},{4,8},{8,12},{12,16},{16,20},{20,24},{24,28},{28,32},{32,36}... | collective-permute-start | bytes 1572872 | tf_op jit(solution)/shard_map/while/body/eval_jaxpr/ppermute | solution.py:16
  343.7 12.9 %collective-permute-start = (bf16[256,1024]{0,1:T(8,128)(2,1)}, bf16[256,1024]{0,1:T(8,128)(2,1)}, u32[]{:S(2)}, u32[]{:S(2)}) collective-permute-start(bf16[256,1024]{0,1:T(8,128)(2,1)} %copy.132), channel_id=1, source_target_pairs={{0,4},{4,8},{8,12},{12,16},{16,20},{20,24},{24,28},{28,32},{32,36}... | collective-permute-start | bytes 1572872 | tf_op jit(solution)/shard_map/while/body/eval_jaxpr/ppermute | solution.py:16
  358.4 12.9 %collective-permute-start = (bf16[256,1024]{0,1:T(8,128)(2,1)}, bf16[256,1024]{0,1:T(8,128)(2,1)}, u32[]{:S(2)}, u32[]{:S(2)}) collective-permute-start(bf16[256,1024]{0,1:T(8,128)(2,1)} %copy.132), channel_id=1, source_target_pairs={{0,4},{4,8},{8,12},{12,16},{16,20},{20,24},{24,28},{28,32},{32,36}... | collective-permute-start | bytes 1572872 | tf_op jit(solution)/shard_map/while/body/eval_jaxpr/ppermute | solution.py:16
  373.2 12.9 %collective-permute-start = (bf16[256,1024]{0,1:T(8,128)(2,1)}, bf16[256,1024]{0,1:T(8,128)(2,1)}, u32[]{:S(2)}, u32[]{:S(2)}) collective-permute-start(bf16[256,1024]{0,1:T(8,128)(2,1)} %copy.132), channel_id=1, source_target_pairs={{0,4},{4,8},{8,12},{12,16},{16,20},{20,24},{24,28},{28,32},{32,36}... | collective-permute-start | bytes 1572872 | tf_op jit(solution)/shard_map/while/body/eval_jaxpr/ppermute | solution.py:16
  388.0 12.9 %collective-permute-start = (bf16[256,1024]{0,1:T(8,128)(2,1)}, bf16[256,1024]{0,1:T(8,128)(2,1)}, u32[]{:S(2)}, u32[]{:S(2)}) collective-permute-start(bf16[256,1024]{0,1:T(8,128)(2,1)} %copy.132), channel_id=1, source_target_pairs={{0,4},{4,8},{8,12},{12,16},{16,20},{20,24},{24,28},{28,32},{32,36}... | collective-permute-start | bytes 1572872 | tf_op jit(solution)/shard_map/while/body/eval_jaxpr/ppermute | solution.py:16
  402.8 12.9 %collective-permute-start = (bf16[256,1024]{0,1:T(8,128)(2,1)}, bf16[256,1024]{0,1:T(8,128)(2,1)}, u32[]{:S(2)}, u32[]{:S(2)}) collective-permute-start(bf16[256,1024]{0,1:T(8,128)(2,1)} %copy.132), channel_id=1, source_target_pairs={{0,4},{4,8},{8,12},{12,16},{16,20},{20,24},{24,28},{28,32},{32,36}... | collective-permute-start | bytes 1572872 | tf_op jit(solution)/shard_map/while/body/eval_jaxpr/ppermute | solution.py:16
  417.6 12.9 %collective-permute-start = (bf16[256,1024]{0,1:T(8,128)(2,1)}, bf16[256,1024]{0,1:T(8,128)(2,1)}, u32[]{:S(2)}, u32[]{:S(2)}) collective-permute-start(bf16[256,1024]{0,1:T(8,128)(2,1)} %copy.132), channel_id=1, source_target_pairs={{0,4},{4,8},{8,12},{12,16},{16,20},{20,24},{24,28},{28,32},{32,36}... | collective-permute-start | bytes 1572872 | tf_op jit(solution)/shard_map/while/body/eval_jaxpr/ppermute | solution.py:16
  432.4 12.9 %collective-permute-start = (bf16[256,1024]{0,1:T(8,128)(2,1)}, bf16[256,1024]{0,1:T(8,128)(2,1)}, u32[]{:S(2)}, u32[]{:S(2)}) collective-permute-start(bf16[256,1024]{0,1:T(8,128)(2,1)} %copy.132), channel_id=1, source_target_pairs={{0,4},{4,8},{8,12},{12,16},{16,20},{20,24},{24,28},{28,32},{32,36}... | collective-permute-start | bytes 1572872 | tf_op jit(solution)/shard_map/while/body/eval_jaxpr/ppermute | solution.py:16
  447.1 12.9 %collective-permute-start = (bf16[256,1024]{0,1:T(8,128)(2,1)}, bf16[256,1024]{0,1:T(8,128)(2,1)}, u32[]{:S(2)}, u32[]{:S(2)}) collective-permute-start(bf16[256,1024]{0,1:T(8,128)(2,1)} %copy.132), channel_id=1, source_target_pairs={{0,4},{4,8},{8,12},{12,16},{16,20},{20,24},{24,28},{28,32},{32,36}... | collective-permute-start | bytes 1572872 | tf_op jit(solution)/shard_map/while/body/eval_jaxpr/ppermute | solution.py:16
  (24 other events, 745.9 us)
Sparse Core Ops, SparseCore 0:
  464.9 134.9 all-reduce.1
where the time goes:
time: 615 us; the launch traced here: 609 us
  waiting for transfers between devices  283 us (46%)
  starting transfers between devices  165 us (27%)
  local copies, waits for them, and re-layouts  71.1 us (12%)
  other arithmetic  43.3 us (7%)
  loops' own time  19.5 us (3%)
  between operations  15.7 us (3%)
  matrix products  12.3 us (2%)
    ppermute x32, starting transfers between devices, shifted(): lax.ppermute(value, axis, [(source, source + steps) for source in range(f...  165 us
    ppermute x32, waiting for transfers between devices, shifted(): lax.ppermute(value, axis, [(source, source + steps) for source in range(f...  148 us
    psum x1, waiting for transfers between devices, on_device(): lax.psum(jnp.dot(merged, w_out, preferred_element_type=jnp.float32).astyp...  135 us
    while x31, local copies, waits for them, and re-layouts  57.9 us
    reduce_or x31, other arithmetic, absorb(): return lax.cond(jnp.any(allowed), compute, keep, state)  24.8 us
    another operation x1, loops' own time, on_device(): state, moving = lax.fori_loop(0, reach - 1, turn, (state, arriving))  19 us
  transfers between devices with their start and end apart: 33, of which 32 were waited for; matrix products, arithmetic and copies ran while one was open for 7% of the time, Pallas kernels for 0%

commit v1 on v0

--- a/solution.py
+++ b/solution.py
@@ -128,8 +128,11 @@
         * (1.0 - lambda_start)
     )
     merged = jnp.transpose(normed_heads, (1, 0, 2)).reshape(rows, heads * VD).astype(jnp.bfloat16)
-    summed = lax.psum(
-        jnp.dot(merged, w_out, preferred_element_type=jnp.float32).astype(jnp.bfloat16), "tp"
+    summed = jnp.sum(
+        lax.all_gather(
+            jnp.dot(merged, w_out, preferred_element_type=jnp.float32).astype(jnp.bfloat16), "tp"
+        ),
+        axis=0,
     ).astype(jnp.float32)
     hidden = (xf + summed).astype(jnp.bfloat16)
     return (hidden, key_flat, values)

time: 615 us -> 640 us (1.041)
  the two profiles are of different devices: /device:TPU:1 before, /device:TPU:37 now
where the time goes in v1:
time: 640 us; the launch traced here: 634 us
  starting transfers between devices  213 us (33%)
  waiting for transfers between devices  201 us (31%)
  local copies, waits for them, and re-layouts  92.2 us (14%)
  other arithmetic  67.6 us (11%)
  matrix products  25.3 us (4%)
  loops' own time  19.7 us (3%)
  between operations  15.6 us (2%)
    ppermute x32, starting transfers between devices, shifted(): lax.ppermute(value, axis, [(source, source + steps) for source in range(f...  213 us
    all_gather x1, waiting for transfers between devices, on_device(): lax.all_gather(jnp.dot(merged, w_out, preferred_element_type=jnp.float32)...  106 us
    ppermute x32, waiting for transfers between devices, shifted(): lax.ppermute(value, axis, [(source, source + steps) for source in range(f...  95.7 us
    while x31, local copies, waits for them, and re-layouts  57.9 us
    reduce_or x31, other arithmetic, absorb(): return lax.cond(jnp.any(allowed), compute, keep, state)  24.8 us
    another operation x1, loops' own time, on_device(): state, moving = lax.fori_loop(0, reach - 1, turn, (state, arriving))  19 us
    slice x13, local copies, waits for them, and re-layouts, compute(): shard_values = shard[:, key_cols:].reshape(rows, heads, VD)  13.9 us
  transfers between devices with their start and end apart: 33, of which 32 were waited for; matrix products, arithmetic and copies ran while one was open for 15% of the time, Pallas kernels for 0%

profile of v1, /device:TPU:37, one launch (start us, length us, event | category | flops | bytes accessed | tf_op | source)
XLA Modules:
  0.0 634.2 jit_solution(6324126706851802144)
XLA Ops:
  43.8 466.3 %while.23 = (s32[]{:T(128)}, f32[2,2,256]{2,1,0:T(2,128)}, f32[2,2,256]{2,1,0:T(2,128)S(1)}, f32[2,2,256,256]{3,2,0,1:T(8,128)S(1)}, bf16[256,1024]{0,1:T(8,128)...) while((s32[]{:T(128)}, f32[2,2,256]{2,1,0:T(2,128)}, ...), condition=%wide.region_19.20_spmd.clone.clone, body=%wide.region_12.19_spmd.clone.clone.sunk | while | flops 204019456 | bytes 10498871 | solution.py:119
  108.3 7.4 %collective-permute-start = (bf16[256,1024]{0,1:T(8,128)(2,1)}, bf16[256,1024]{0,1:T(8,128)(2,1)}, u32[]{:S(2)}, u32[]{:S(2)}) collective-permute-start(bf16[256,1024]{0,1:T(8,128)(2,1)} %copy.132), channel_id=1, source_target_pairs={{0,4},{4,8},{8,12},{12,16},{16,20},{20,24},{24,28},{28,32},{32,36}... | collective-permute-start | bytes 1572872 | tf_op jit(solution)/shard_map/while/body/eval_jaxpr/ppermute | solution.py:16
  124.0 7.4 %collective-permute-start = (bf16[256,1024]{0,1:T(8,128)(2,1)}, bf16[256,1024]{0,1:T(8,128)(2,1)}, u32[]{:S(2)}, u32[]{:S(2)}) collective-permute-start(bf16[256,1024]{0,1:T(8,128)(2,1)} %copy.132), channel_id=1, source_target_pairs={{0,4},{4,8},{8,12},{12,16},{16,20},{20,24},{24,28},{28,32},{32,36}... | collective-permute-start | bytes 1572872 | tf_op jit(solution)/shard_map/while/body/eval_jaxpr/ppermute | solution.py:16
  139.6 7.4 %collective-permute-start = (bf16[256,1024]{0,1:T(8,128)(2,1)}, bf16[256,1024]{0,1:T(8,128)(2,1)}, u32[]{:S(2)}, u32[]{:S(2)}) collective-permute-start(bf16[256,1024]{0,1:T(8,128)(2,1)} %copy.132), channel_id=1, source_target_pairs={{0,4},{4,8},{8,12},{12,16},{16,20},{20,24},{24,28},{28,32},{32,36}... | collective-permute-start | bytes 1572872 | tf_op jit(solution)/shard_map/while/body/eval_jaxpr/ppermute | solution.py:16
  155.3 7.4 %collective-permute-start = (bf16[256,1024]{0,1:T(8,128)(2,1)}, bf16[256,1024]{0,1:T(8,128)(2,1)}, u32[]{:S(2)}, u32[]{:S(2)}) collective-permute-start(bf16[256,1024]{0,1:T(8,128)(2,1)} %copy.132), channel_id=1, source_target_pairs={{0,4},{4,8},{8,12},{12,16},{16,20},{20,24},{24,28},{28,32},{32,36}... | collective-permute-start | bytes 1572872 | tf_op jit(solution)/shard_map/while/body/eval_jaxpr/ppermute | solution.py:16
  171.0 7.4 %collective-permute-start = (bf16[256,1024]{0,1:T(8,128)(2,1)}, bf16[256,1024]{0,1:T(8,128)(2,1)}, u32[]{:S(2)}, u32[]{:S(2)}) collective-permute-start(bf16[256,1024]{0,1:T(8,128)(2,1)} %copy.132), channel_id=1, source_target_pairs={{0,4},{4,8},{8,12},{12,16},{16,20},{20,24},{24,28},{28,32},{32,36}... | collective-permute-start | bytes 1572872 | tf_op jit(solution)/shard_map/while/body/eval_jaxpr/ppermute | solution.py:16
  202.4 7.4 %collective-permute-start = (bf16[256,1024]{0,1:T(8,128)(2,1)}, bf16[256,1024]{0,1:T(8,128)(2,1)}, u32[]{:S(2)}, u32[]{:S(2)}) collective-permute-start(bf16[256,1024]{0,1:T(8,128)(2,1)} %copy.132), channel_id=1, source_target_pairs={{0,4},{4,8},{8,12},{12,16},{16,20},{20,24},{24,28},{28,32},{32,36}... | collective-permute-start | bytes 1572872 | tf_op jit(solution)/shard_map/while/body/eval_jaxpr/ppermute | solution.py:16
  218.0 7.4 %collective-permute-start = (bf16[256,1024]{0,1:T(8,128)(2,1)}, bf16[256,1024]{0,1:T(8,128)(2,1)}, u32[]{:S(2)}, u32[]{:S(2)}) collective-permute-start(bf16[256,1024]{0,1:T(8,128)(2,1)} %copy.132), channel_id=1, source_target_pairs={{0,4},{4,8},{8,12},{12,16},{16,20},{20,24},{24,28},{28,32},{32,36}... | collective-permute-start | bytes 1572872 | tf_op jit(solution)/shard_map/while/body/eval_jaxpr/ppermute | solution.py:16
  249.4 7.4 %collective-permute-start = (bf16[256,1024]{0,1:T(8,128)(2,1)}, bf16[256,1024]{0,1:T(8,128)(2,1)}, u32[]{:S(2)}, u32[]{:S(2)}) collective-permute-start(bf16[256,1024]{0,1:T(8,128)(2,1)} %copy.132), channel_id=1, source_target_pairs={{0,4},{4,8},{8,12},{12,16},{16,20},{20,24},{24,28},{28,32},{32,36}... | collective-permute-start | bytes 1572872 | tf_op jit(solution)/shard_map/while/body/eval_jaxpr/ppermute | solution.py:16
  292.4 7.4 %collective-permute-start = (bf16[256,1024]{0,1:T(8,128)(2,1)}, bf16[256,1024]{0,1:T(8,128)(2,1)}, u32[]{:S(2)}, u32[]{:S(2)}) collective-permute-start(bf16[256,1024]{0,1:T(8,128)(2,1)} %copy.132), channel_id=1, source_target_pairs={{0,4},{4,8},{8,12},{12,16},{16,20},{20,24},{24,28},{28,32},{32,36}... | collective-permute-start | bytes 1572872 | tf_op jit(solution)/shard_map/while/body/eval_jaxpr/ppermute | solution.py:16
  308.1 7.4 %collective-permute-start = (bf16[256,1024]{0,1:T(8,128)(2,1)}, bf16[256,1024]{0,1:T(8,128)(2,1)}, u32[]{:S(2)}, u32[]{:S(2)}) collective-permute-start(bf16[256,1024]{0,1:T(8,128)(2,1)} %copy.132), channel_id=1, source_target_pairs={{0,4},{4,8},{8,12},{12,16},{16,20},{20,24},{24,28},{28,32},{32,36}... | collective-permute-start | bytes 1572872 | tf_op jit(solution)/shard_map/while/body/eval_jaxpr/ppermute | solution.py:16
  323.8 7.4 %collective-permute-start = (bf16[256,1024]{0,1:T(8,128)(2,1)}, bf16[256,1024]{0,1:T(8,128)(2,1)}, u32[]{:S(2)}, u32[]{:S(2)}) collective-permute-start(bf16[256,1024]{0,1:T(8,128)(2,1)} %copy.132), channel_id=1, source_target_pairs={{0,4},{4,8},{8,12},{12,16},{16,20},{20,24},{24,28},{28,32},{32,36}... | collective-permute-start | bytes 1572872 | tf_op jit(solution)/shard_map/while/body/eval_jaxpr/ppermute | solution.py:16
  339.5 7.4 %collective-permute-start = (bf16[256,1024]{0,1:T(8,128)(2,1)}, bf16[256,1024]{0,1:T(8,128)(2,1)}, u32[]{:S(2)}, u32[]{:S(2)}) collective-permute-start(bf16[256,1024]{0,1:T(8,128)(2,1)} %copy.132), channel_id=1, source_target_pairs={{0,4},{4,8},{8,12},{12,16},{16,20},{20,24},{24,28},{28,32},{32,36}... | collective-permute-start | bytes 1572872 | tf_op jit(solution)/shard_map/while/body/eval_jaxpr/ppermute | solution.py:16
  355.2 7.4 %collective-permute-start = (bf16[256,1024]{0,1:T(8,128)(2,1)}, bf16[256,1024]{0,1:T(8,128)(2,1)}, u32[]{:S(2)}, u32[]{:S(2)}) collective-permute-start(bf16[256,1024]{0,1:T(8,128)(2,1)} %copy.132), channel_id=1, source_target_pairs={{0,4},{4,8},{8,12},{12,16},{16,20},{20,24},{24,28},{28,32},{32,36}... | collective-permute-start | bytes 1572872 | tf_op jit(solution)/shard_map/while/body/eval_jaxpr/ppermute | solution.py:16
  370.9 7.4 %collective-permute-start = (bf16[256,1024]{0,1:T(8,128)(2,1)}, bf16[256,1024]{0,1:T(8,128)(2,1)}, u32[]{:S(2)}, u32[]{:S(2)}) collective-permute-start(bf16[256,1024]{0,1:T(8,128)(2,1)} %copy.132), channel_id=1, source_target_pairs={{0,4},{4,8},{8,12},{12,16},{16,20},{20,24},{24,28},{28,32},{32,36}... | collective-permute-start | bytes 1572872 | tf_op jit(solution)/shard_map/while/body/eval_jaxpr/ppermute | solution.py:16
  386.5 7.4 %collective-permute-start = (bf16[256,1024]{0,1:T(8,128)(2,1)}, bf16[256,1024]{0,1:T(8,128)(2,1)}, u32[]{:S(2)}, u32[]{:S(2)}) collective-permute-start(bf16[256,1024]{0,1:T(8,128)(2,1)} %copy.132), channel_id=1, source_target_pairs={{0,4},{4,8},{8,12},{12,16},{16,20},{20,24},{24,28},{28,32},{32,36}... | collective-permute-start | bytes 1572872 | tf_op jit(solution)/shard_map/while/body/eval_jaxpr/ppermute | solution.py:16
  402.2 7.4 %collective-permute-start = (bf16[256,1024]{0,1:T(8,128)(2,1)}, bf16[256,1024]{0,1:T(8,128)(2,1)}, u32[]{:S(2)}, u32[]{:S(2)}) collective-permute-start(bf16[256,1024]{0,1:T(8,128)(2,1)} %copy.132), channel_id=1, source_target_pairs={{0,4},{4,8},{8,12},{12,16},{16,20},{20,24},{24,28},{28,32},{32,36}... | collective-permute-start | bytes 1572872 | tf_op jit(solution)/shard_map/while/body/eval_jaxpr/ppermute | solution.py:16
  417.9 7.4 %collective-permute-start = (bf16[256,1024]{0,1:T(8,128)(2,1)}, bf16[256,1024]{0,1:T(8,128)(2,1)}, u32[]{:S(2)}, u32[]{:S(2)}) collective-permute-start(bf16[256,1024]{0,1:T(8,128)(2,1)} %copy.132), channel_id=1, source_target_pairs={{0,4},{4,8},{8,12},{12,16},{16,20},{20,24},{24,28},{28,32},{32,36}... | collective-permute-start | bytes 1572872 | tf_op jit(solution)/shard_map/while/body/eval_jaxpr/ppermute | solution.py:16
  433.6 7.4 %collective-permute-start = (bf16[256,1024]{0,1:T(8,128)(2,1)}, bf16[256,1024]{0,1:T(8,128)(2,1)}, u32[]{:S(2)}, u32[]{:S(2)}) collective-permute-start(bf16[256,1024]{0,1:T(8,128)(2,1)} %copy.132), channel_id=1, source_target_pairs={{0,4},{4,8},{8,12},{12,16},{16,20},{20,24},{24,28},{28,32},{32,36}... | collective-permute-start | bytes 1572872 | tf_op jit(solution)/shard_map/while/body/eval_jaxpr/ppermute | solution.py:16
  449.3 7.4 %collective-permute-start = (bf16[256,1024]{0,1:T(8,128)(2,1)}, bf16[256,1024]{0,1:T(8,128)(2,1)}, u32[]{:S(2)}, u32[]{:S(2)}) collective-permute-start(bf16[256,1024]{0,1:T(8,128)(2,1)} %copy.132), channel_id=1, source_target_pairs={{0,4},{4,8},{8,12},{12,16},{16,20},{20,24},{24,28},{28,32},{32,36}... | collective-permute-start | bytes 1572872 | tf_op jit(solution)/shard_map/while/body/eval_jaxpr/ppermute | solution.py:16
  465.0 7.4 %collective-permute-start = (bf16[256,1024]{0,1:T(8,128)(2,1)}, bf16[256,1024]{0,1:T(8,128)(2,1)}, u32[]{:S(2)}, u32[]{:S(2)}) collective-permute-start(bf16[256,1024]{0,1:T(8,128)(2,1)} %copy.132), channel_id=1, source_target_pairs={{0,4},{4,8},{8,12},{12,16},{16,20},{20,24},{24,28},{28,32},{32,36}... | collective-permute-start | bytes 1572872 | tf_op jit(solution)/shard_map/while/body/eval_jaxpr/ppermute | solution.py:16
  480.6 7.4 %collective-permute-start = (bf16[256,1024]{0,1:T(8,128)(2,1)}, bf16[256,1024]{0,1:T(8,128)(2,1)}, u32[]{:S(2)}, u32[]{:S(2)}) collective-permute-start(bf16[256,1024]{0,1:T(8,128)(2,1)} %copy.132), channel_id=1, source_target_pairs={{0,4},{4,8},{8,12},{12,16},{16,20},{20,24},{24,28},{28,32},{32,36}... | collective-permute-start | bytes 1572872 | tf_op jit(solution)/shard_map/while/body/eval_jaxpr/ppermute | solution.py:16
  496.3 7.4 %collective-permute-start = (bf16[256,1024]{0,1:T(8,128)(2,1)}, bf16[256,1024]{0,1:T(8,128)(2,1)}, u32[]{:S(2)}, u32[]{:S(2)}) collective-permute-start(bf16[256,1024]{0,1:T(8,128)(2,1)} %copy.132), channel_id=1, source_target_pairs={{0,4},{4,8},{8,12},{12,16},{16,20},{20,24},{24,28},{28,32},{32,36}... | collective-permute-start | bytes 1572872 | tf_op jit(solution)/shard_map/while/body/eval_jaxpr/ppermute | solution.py:16
  514.9 105.6 %all-gather.3.cloned.1.call-done = bf16[1024,2048]{1,0:T(8,128)(2,1)} async-done(((bf16[256,2048]{1,0:T(8,128)(2,1)}), bf16[1024,2048]{1,0:T(8,128)(2,1)}) %all-gather.3.cloned.1.call-update) | async-done | bytes 4194320 | tf_op jit(solution)/shard_map/all_gather | solution.py:132
  (444 shorter events, 394.4 us)
Async XLA Ops:
  7.2 613.3 %all-gather.3.cloned.1.call-start = ((), (), s32[]{:S(2)}) async-start(), calls=%async_computation | async-start | bytes 5242880 | tf_op jit(solution)/shard_map/all_gather | solution.py:132
  23.8 18.0 %collective-permute-start.1 = (bf16[256,1024]{1,0:T(8,128)(2,1)}, bf16[256,1024]{1,0:T(8,128)(2,1)}, u32[]{:S(2)}, u32[]{:S(2)}) collective-permute-start(bf16[256,1024]{1,0:T(8,128)(2,1)} %pad_maximum_fusion), channel_id=1, source_target_pairs={{0,4},{4,8},{8,12},{12,16},{16,20},{20,24},{24,28},{28,32},{32,36}... | collective-permute-start | bytes 1572872 | tf_op jit(solution)/shard_map/ppermute | solution.py:16
  108.3 13.8 %collective-permute-start = (bf16[256,1024]{0,1:T(8,128)(2,1)}, bf16[256,1024]{0,1:T(8,128)(2,1)}, u32[]{:S(2)}, u32[]{:S(2)}) collective-permute-start(bf16[256,1024]{0,1:T(8,128)(2,1)} %copy.132), channel_id=1, source_target_pairs={{0,4},{4,8},{8,12},{12,16},{16,20},{20,24},{24,28},{28,32},{32,36}... | collective-permute-start | bytes 1572872 | tf_op jit(solution)/shard_map/while/body/eval_jaxpr/ppermute | solution.py:16
  124.0 13.8 %collective-permute-start = (bf16[256,1024]{0,1:T(8,128)(2,1)}, bf16[256,1024]{0,1:T(8,128)(2,1)}, u32[]{:S(2)}, u32[]{:S(2)}) collective-permute-start(bf16[256,1024]{0,1:T(8,128)(2,1)} %copy.132), channel_id=1, source_target_pairs={{0,4},{4,8},{8,12},{12,16},{16,20},{20,24},{24,28},{28,32},{32,36}... | collective-permute-start | bytes 1572872 | tf_op jit(solution)/shard_map/while/body/eval_jaxpr/ppermute | solution.py:16
  139.6 13.8 %collective-permute-start = (bf16[256,1024]{0,1:T(8,128)(2,1)}, bf16[256,1024]{0,1:T(8,128)(2,1)}, u32[]{:S(2)}, u32[]{:S(2)}) collective-permute-start(bf16[256,1024]{0,1:T(8,128)(2,1)} %copy.132), channel_id=1, source_target_pairs={{0,4},{4,8},{8,12},{12,16},{16,20},{20,24},{24,28},{28,32},{32,36}... | collective-permute-start | bytes 1572872 | tf_op jit(solution)/shard_map/while/body/eval_jaxpr/ppermute | solution.py:16
  155.3 13.8 %collective-permute-start = (bf16[256,1024]{0,1:T(8,128)(2,1)}, bf16[256,1024]{0,1:T(8,128)(2,1)}, u32[]{:S(2)}, u32[]{:S(2)}) collective-permute-start(bf16[256,1024]{0,1:T(8,128)(2,1)} %copy.132), channel_id=1, source_target_pairs={{0,4},{4,8},{8,12},{12,16},{16,20},{20,24},{24,28},{28,32},{32,36}... | collective-permute-start | bytes 1572872 | tf_op jit(solution)/shard_map/while/body/eval_jaxpr/ppermute | solution.py:16
  171.0 13.8 %collective-permute-start = (bf16[256,1024]{0,1:T(8,128)(2,1)}, bf16[256,1024]{0,1:T(8,128)(2,1)}, u32[]{:S(2)}, u32[]{:S(2)}) collective-permute-start(bf16[256,1024]{0,1:T(8,128)(2,1)} %copy.132), channel_id=1, source_target_pairs={{0,4},{4,8},{8,12},{12,16},{16,20},{20,24},{24,28},{28,32},{32,36}... | collective-permute-start | bytes 1572872 | tf_op jit(solution)/shard_map/while/body/eval_jaxpr/ppermute | solution.py:16
  202.4 13.8 %collective-permute-start = (bf16[256,1024]{0,1:T(8,128)(2,1)}, bf16[256,1024]{0,1:T(8,128)(2,1)}, u32[]{:S(2)}, u32[]{:S(2)}) collective-permute-start(bf16[256,1024]{0,1:T(8,128)(2,1)} %copy.132), channel_id=1, source_target_pairs={{0,4},{4,8},{8,12},{12,16},{16,20},{20,24},{24,28},{28,32},{32,36}... | collective-permute-start | bytes 1572872 | tf_op jit(solution)/shard_map/while/body/eval_jaxpr/ppermute | solution.py:16
  218.0 13.8 %collective-permute-start = (bf16[256,1024]{0,1:T(8,128)(2,1)}, bf16[256,1024]{0,1:T(8,128)(2,1)}, u32[]{:S(2)}, u32[]{:S(2)}) collective-permute-start(bf16[256,1024]{0,1:T(8,128)(2,1)} %copy.132), channel_id=1, source_target_pairs={{0,4},{4,8},{8,12},{12,16},{16,20},{20,24},{24,28},{28,32},{32,36}... | collective-permute-start | bytes 1572872 | tf_op jit(solution)/shard_map/while/body/eval_jaxpr/ppermute | solution.py:16
  249.4 13.8 %collective-permute-start = (bf16[256,1024]{0,1:T(8,128)(2,1)}, bf16[256,1024]{0,1:T(8,128)(2,1)}, u32[]{:S(2)}, u32[]{:S(2)}) collective-permute-start(bf16[256,1024]{0,1:T(8,128)(2,1)} %copy.132), channel_id=1, source_target_pairs={{0,4},{4,8},{8,12},{12,16},{16,20},{20,24},{24,28},{28,32},{32,36}... | collective-permute-start | bytes 1572872 | tf_op jit(solution)/shard_map/while/body/eval_jaxpr/ppermute | solution.py:16
  292.4 13.8 %collective-permute-start = (bf16[256,1024]{0,1:T(8,128)(2,1)}, bf16[256,1024]{0,1:T(8,128)(2,1)}, u32[]{:S(2)}, u32[]{:S(2)}) collective-permute-start(bf16[256,1024]{0,1:T(8,128)(2,1)} %copy.132), channel_id=1, source_target_pairs={{0,4},{4,8},{8,12},{12,16},{16,20},{20,24},{24,28},{28,32},{32,36}... | collective-permute-start | bytes 1572872 | tf_op jit(solution)/shard_map/while/body/eval_jaxpr/ppermute | solution.py:16
  308.1 13.8 %collective-permute-start = (bf16[256,1024]{0,1:T(8,128)(2,1)}, bf16[256,1024]{0,1:T(8,128)(2,1)}, u32[]{:S(2)}, u32[]{:S(2)}) collective-permute-start(bf16[256,1024]{0,1:T(8,128)(2,1)} %copy.132), channel_id=1, source_target_pairs={{0,4},{4,8},{8,12},{12,16},{16,20},{20,24},{24,28},{28,32},{32,36}... | collective-permute-start | bytes 1572872 | tf_op jit(solution)/shard_map/while/body/eval_jaxpr/ppermute | solution.py:16
  323.8 13.8 %collective-permute-start = (bf16[256,1024]{0,1:T(8,128)(2,1)}, bf16[256,1024]{0,1:T(8,128)(2,1)}, u32[]{:S(2)}, u32[]{:S(2)}) collective-permute-start(bf16[256,1024]{0,1:T(8,128)(2,1)} %copy.132), channel_id=1, source_target_pairs={{0,4},{4,8},{8,12},{12,16},{16,20},{20,24},{24,28},{28,32},{32,36}... | collective-permute-start | bytes 1572872 | tf_op jit(solution)/shard_map/while/body/eval_jaxpr/ppermute | solution.py:16
  339.5 13.8 %collective-permute-start = (bf16[256,1024]{0,1:T(8,128)(2,1)}, bf16[256,1024]{0,1:T(8,128)(2,1)}, u32[]{:S(2)}, u32[]{:S(2)}) collective-permute-start(bf16[256,1024]{0,1:T(8,128)(2,1)} %copy.132), channel_id=1, source_target_pairs={{0,4},{4,8},{8,12},{12,16},{16,20},{20,24},{24,28},{28,32},{32,36}... | collective-permute-start | bytes 1572872 | tf_op jit(solution)/shard_map/while/body/eval_jaxpr/ppermute | solution.py:16
  355.2 13.8 %collective-permute-start = (bf16[256,1024]{0,1:T(8,128)(2,1)}, bf16[256,1024]{0,1:T(8,128)(2,1)}, u32[]{:S(2)}, u32[]{:S(2)}) collective-permute-start(bf16[256,1024]{0,1:T(8,128)(2,1)} %copy.132), channel_id=1, source_target_pairs={{0,4},{4,8},{8,12},{12,16},{16,20},{20,24},{24,28},{28,32},{32,36}... | collective-permute-start | bytes 1572872 | tf_op jit(solution)/shard_map/while/body/eval_jaxpr/ppermute | solution.py:16
  370.9 13.8 %collective-permute-start = (bf16[256,1024]{0,1:T(8,128)(2,1)}, bf16[256,1024]{0,1:T(8,128)(2,1)}, u32[]{:S(2)}, u32[]{:S(2)}) collective-permute-start(bf16[256,1024]{0,1:T(8,128)(2,1)} %copy.132), channel_id=1, source_target_pairs={{0,4},{4,8},{8,12},{12,16},{16,20},{20,24},{24,28},{28,32},{32,36}... | collective-permute-start | bytes 1572872 | tf_op jit(solution)/shard_map/while/body/eval_jaxpr/ppermute | solution.py:16
  386.5 13.8 %collective-permute-start = (bf16[256,1024]{0,1:T(8,128)(2,1)}, bf16[256,1024]{0,1:T(8,128)(2,1)}, u32[]{:S(2)}, u32[]{:S(2)}) collective-permute-start(bf16[256,1024]{0,1:T(8,128)(2,1)} %copy.132), channel_id=1, source_target_pairs={{0,4},{4,8},{8,12},{12,16},{16,20},{20,24},{24,28},{28,32},{32,36}... | collective-permute-start | bytes 1572872 | tf_op jit(solution)/shard_map/while/body/eval_jaxpr/ppermute | solution.py:16
  402.2 13.8 %collective-permute-start = (bf16[256,1024]{0,1:T(8,128)(2,1)}, bf16[256,1024]{0,1:T(8,128)(2,1)}, u32[]{:S(2)}, u32[]{:S(2)}) collective-permute-start(bf16[256,1024]{0,1:T(8,128)(2,1)} %copy.132), channel_id=1, source_target_pairs={{0,4},{4,8},{8,12},{12,16},{16,20},{20,24},{24,28},{28,32},{32,36}... | collective-permute-start | bytes 1572872 | tf_op jit(solution)/shard_map/while/body/eval_jaxpr/ppermute | solution.py:16
  417.9 13.8 %collective-permute-start = (bf16[256,1024]{0,1:T(8,128)(2,1)}, bf16[256,1024]{0,1:T(8,128)(2,1)}, u32[]{:S(2)}, u32[]{:S(2)}) collective-permute-start(bf16[256,1024]{0,1:T(8,128)(2,1)} %copy.132), channel_id=1, source_target_pairs={{0,4},{4,8},{8,12},{12,16},{16,20},{20,24},{24,28},{28,32},{32,36}... | collective-permute-start | bytes 1572872 | tf_op jit(solution)/shard_map/while/body/eval_jaxpr/ppermute | solution.py:16
  433.6 13.8 %collective-permute-start = (bf16[256,1024]{0,1:T(8,128)(2,1)}, bf16[256,1024]{0,1:T(8,128)(2,1)}, u32[]{:S(2)}, u32[]{:S(2)}) collective-permute-start(bf16[256,1024]{0,1:T(8,128)(2,1)} %copy.132), channel_id=1, source_target_pairs={{0,4},{4,8},{8,12},{12,16},{16,20},{20,24},{24,28},{28,32},{32,36}... | collective-permute-start | bytes 1572872 | tf_op jit(solution)/shard_map/while/body/eval_jaxpr/ppermute | solution.py:16
  449.3 13.8 %collective-permute-start = (bf16[256,1024]{0,1:T(8,128)(2,1)}, bf16[256,1024]{0,1:T(8,128)(2,1)}, u32[]{:S(2)}, u32[]{:S(2)}) collective-permute-start(bf16[256,1024]{0,1:T(8,128)(2,1)} %copy.132), channel_id=1, source_target_pairs={{0,4},{4,8},{8,12},{12,16},{16,20},{20,24},{24,28},{28,32},{32,36}... | collective-permute-start | bytes 1572872 | tf_op jit(solution)/shard_map/while/body/eval_jaxpr/ppermute | solution.py:16
  465.0 13.8 %collective-permute-start = (bf16[256,1024]{0,1:T(8,128)(2,1)}, bf16[256,1024]{0,1:T(8,128)(2,1)}, u32[]{:S(2)}, u32[]{:S(2)}) collective-permute-start(bf16[256,1024]{0,1:T(8,128)(2,1)} %copy.132), channel_id=1, source_target_pairs={{0,4},{4,8},{8,12},{12,16},{16,20},{20,24},{24,28},{28,32},{32,36}... | collective-permute-start | bytes 1572872 | tf_op jit(solution)/shard_map/while/body/eval_jaxpr/ppermute | solution.py:16
  480.6 13.8 %collective-permute-start = (bf16[256,1024]{0,1:T(8,128)(2,1)}, bf16[256,1024]{0,1:T(8,128)(2,1)}, u32[]{:S(2)}, u32[]{:S(2)}) collective-permute-start(bf16[256,1024]{0,1:T(8,128)(2,1)} %copy.132), channel_id=1, source_target_pairs={{0,4},{4,8},{8,12},{12,16},{16,20},{20,24},{24,28},{28,32},{32,36}... | collective-permute-start | bytes 1572872 | tf_op jit(solution)/shard_map/while/body/eval_jaxpr/ppermute | solution.py:16
  496.3 13.8 %collective-permute-start = (bf16[256,1024]{0,1:T(8,128)(2,1)}, bf16[256,1024]{0,1:T(8,128)(2,1)}, u32[]{:S(2)}, u32[]{:S(2)}) collective-permute-start(bf16[256,1024]{0,1:T(8,128)(2,1)} %copy.132), channel_id=1, source_target_pairs={{0,4},{4,8},{8,12},{12,16},{16,20},{20,24},{24,28},{28,32},{32,36}... | collective-permute-start | bytes 1572872 | tf_op jit(solution)/shard_map/while/body/eval_jaxpr/ppermute | solution.py:16
  (25 other events, 666.7 us)
Sparse Core Ops, SparseCore 0:
  515.0 105.4 all-gather.2
